TPU v7x, 256 devices: a whole 4x4x8 slice. The times are simulated.
256 devices in a mesh: dp: 8 (over y, core), mp: 32 (over z, x).
Axes of the slice: x: 4, y: 4, z: 8, core: 2. Of those that a mesh axis runs over, the one named last changes fastest.
Arguments:
- table: bfloat16 [32, 2048, 128], P('mp'), may hold values from -6 to 6
- ids: int32 [65536, 32, 2], P('dp', 'mp'), may hold values from 0 to 2047
- counts: int32 [256, 8], P(('dp', 'mp')), may hold values from 1 to 96, 256 in all within a row
- labels: int32 [65536], P(('dp', 'mp')), may hold values from 0 to 4
- request_home: int32 [2048], replicated, may hold values from 0 to 2047, each once
- user_codes: bfloat16 [2048, 1024], P('dp'), may hold values from -6 to 6
- cross_down: bfloat16 [4096, 256], replicated, may hold values from -0.09375 to 0.09375
- cross_up: bfloat16 [256, 4096], replicated, may hold values from -0.375 to 0.375
- cross_bias: float32 [4096], replicated, may hold values from -4 to 4
- tower_weight: bfloat16 [4096, 1024], P('mp'), may hold values from -0.09375 to 0.09375
- tower_bias: float32 [1024], replicated, may hold values from -3 to 3
Outputs:
- scores: float32 [65536], P(('dp', 'mp'))
- pooled_grad: bfloat16 [65536, 32, 128], P('dp', 'mp')
Inputs may be any that keep to these rules, and one draw needn't show every extreme that they name: `counts`: each row sums to 256; its largest entry is exactly 96. `request_home`: a permutation of the request slots.
All inputs are finite; a program needn't handle non-finite values.
Results may differ from a plain program's by a relative error of at most 0.0097.
Values may be sent and summed in bfloat16 or wider, within the bound.
No kernel may reach another device: no remote copies, remote signals or barrier semaphores. Data moves between devices by JAX's collectives and lax.ppermute only.
A program may use at most 128 MiB of HBM per device.

v0:
```python
import jax
import jax.numpy as jnp
from jax import lax
from jax.sharding import PartitionSpec as P


def members(counts_row, rows):
    ends = jnp.cumsum(counts_row)
    starts = ends - counts_row
    place = jnp.arange(rows, dtype=jnp.int32)[:, None]
    return (place >= starts[None, :]) & (place < ends[None, :])


def dot_last(left, right):
    return lax.dot_general(
        left, right, (((1,), (1,)), ((), ())), preferred_element_type=jnp.float32
    )


def pair_grad(scores, member, labels):
    gain = jnp.exp2(labels.astype(jnp.float32))
    member_f = member.astype(jnp.float32)
    same = jnp.dot(member_f, member_f.T) > 0.5
    diff = gain[:, None] - gain[None, :]
    gap = scores[None, :] - scores[:, None]
    turn = jnp.where(diff > 0, jax.nn.sigmoid(gap), jax.nn.sigmoid(-gap))
    total = jnp.sum(jnp.where(same, diff * turn, 0.0), axis=1)
    seg_gain = jnp.sum(jnp.where(member, (gain - 1.0)[:, None], 0.0), axis=0)
    norm = jnp.sum(jnp.where(member, seg_gain[None, :], 0.0), axis=1)
    return -total / jnp.maximum(norm, 1.0)


def local(
    table,
    ids,
    counts,
    labels,
    request_home,
    user_codes,
    cross_down,
    cross_up,
    cross_bias,
    tower_weight,
    tower_bias,
):
    f32, bf16 = (jnp.float32, jnp.bfloat16)
    n_mp = lax.axis_size("mp")
    n_dp = lax.axis_size("dp")
    d_idx = lax.axis_index("dp")
    m_idx = lax.axis_index("mp")
    rows = labels.shape[0]
    seg_count = counts.shape[1]
    width = user_codes.shape[1]
    emb = table.shape[2]
    rank = cross_down.shape[1]
    scale = 1.0 / jnp.sqrt(jnp.float32(width))
    piece = tower_weight.shape[1] // n_dp
    w_piece = lax.dynamic_slice_in_dim(tower_weight, d_idx * piece, piece, axis=1)
    w_cols = lax.all_gather(w_piece, "mp", axis=0, tiled=True)
    w_all = lax.all_gather(w_cols, "dp", axis=1, tiled=True)
    w3 = w_all.reshape(n_mp, emb, width)
    held = user_codes.shape[0]
    home_local = lax.dynamic_slice_in_dim(request_home, d_idx * held, held)
    wanted = (
        (jnp.arange(n_dp, dtype=jnp.int32)[:, None] * n_mp + m_idx) * seg_count
        + jnp.arange(seg_count, dtype=jnp.int32)[None, :]
    ).reshape(-1)
    pick = (home_local[None, :] == wanted[:, None]).astype(bf16)
    mine = jnp.dot(pick, user_codes, preferred_element_type=f32).astype(bf16)
    user_seg = lax.psum_scatter(
        mine.reshape(n_dp, seg_count, width), "dp", scatter_dimension=0, tiled=False
    )
    slab = table[0]
    picked = jnp.take(slab, ids[:, 0, :], axis=0, mode="clip")
    pooled = jnp.sum(picked.astype(f32), axis=1).astype(bf16)
    x0f = lax.all_to_all(
        pooled.reshape(n_mp, rows, emb), "mp", split_axis=0, concat_axis=0, tiled=True
    )
    member = members(counts[0], rows)
    cd3 = cross_down.reshape(n_mp, emb, rank)
    cu3 = cross_up.reshape(rank, n_mp, emb)
    bias3 = cross_bias.reshape(n_mp, 1, emb)
    z = jnp.einsum("fcd,fdr->cr", x0f, cd3, preferred_element_type=f32).astype(bf16)
    cross = jnp.einsum("cr,rfd->fcd", z, cu3, preferred_element_type=f32) + bias3
    x1 = (x0f * cross + x0f).astype(bf16)
    act = jnp.einsum("fcd,fdh->ch", x1, w3, preferred_element_type=f32) + tower_bias
    sig = jax.nn.sigmoid(act)
    hidden = (act * sig).astype(bf16)
    pair = dot_last(hidden, user_seg)
    score = jnp.sum(jnp.where(member, pair, 0.0), axis=1) * scale
    dscore = pair_grad(score, member, labels)
    code = jnp.dot(member.astype(bf16), user_seg, preferred_element_type=f32)
    slope = sig * (1.0 + act * (1.0 - sig))
    dact = (dscore[:, None] * code * scale * slope).astype(bf16)
    dx1 = jnp.einsum("ch,fdh->fcd", dact, w3, preferred_element_type=f32)
    dcross = (dx1 * x0f).astype(bf16)
    dz = jnp.einsum("fcd,rfd->cr", dcross, cu3, preferred_element_type=f32).astype(bf16)
    dx0 = dx1 * (1.0 + cross) + jnp.einsum("cr,fdr->fcd", dz, cd3, preferred_element_type=f32)
    grads = dx0.astype(bf16)
    returned = lax.all_to_all(grads, "mp", split_axis=0, concat_axis=0, tiled=True)
    return (score, returned.reshape(n_mp * rows, 1, emb))


def solution(mesh):
    in_specs = (
        P("mp", None, None),
        P("dp", "mp", None),
        P(("dp", "mp"), None),
        P(("dp", "mp")),
        P(),
        P("dp", None),
        P(),
        P(),
        P(),
        P("mp", None),
        P(),
    )
    out_specs = (P(("dp", "mp")), P("dp", "mp", None))
    return jax.shard_map(local, mesh=mesh, in_specs=in_specs, out_specs=out_specs, check_vma=False)
```

profile of v0, /device:TPU:10, one launch (start us, length us, event | category | flops | bytes accessed | tf_op | source)
XLA Modules:
  0.0 346.3 jit_solution(14947742715400940034)
XLA Ops:
  7.2 0.0 copy-start
  7.2 0.0 all-gather.3.cloned.1.call-start
  7.2 1.5 constant_dynamic-slice_fusion
  8.7 0.0 all-gather.3.cloned.1.call-update
  8.8 0.0 all-gather.5.cloned.1.call-start
  8.8 80.5 %all-gather.3.cloned.1.call-done = bf16[4096,128]{1,0:T(8,128)(2,1)} async-done(((bf16[128,128]{1,0:T(8,128)(2,1)}), bf16[4096,128]{1,0:T(8,128)(2,1)}) %all-gather.3.cloned.1.call-update) | async-done | bytes 1048592 | tf_op jit(solution)/shard_map/all_gather | solution.py:59
  89.3 0.0 all-gather.5.cloned.1.call-update
  89.3 3.4 copy.18
  92.7 4.1 %reshape.87 = s32[16384]{0:T(1024)S(1)} reshape(s32[8192,1,2]{2,0,1:T(8,128)} %copy.18) | data formatting | bytes 131072 | tf_op jit(solution)/shard_map/jit(_take)/broadcast_in_dim | solution.py:74
  96.8 57.8 %gather_fusion = bf16[16384,128]{1,0:T(8,128)(2,1)} fusion(bf16[2048,128]{1,0:T(8,128)(2,1)S(1)} %bitcast.114, s32[16384]{0:T(1024)S(1)} %broadcast_clamp_fusion), kind=kCustom, calls=%fused_computation | custom fusion | bytes 8454144 | tf_op jit(solution)/shard_map/jit(_take)/gather | solution.py:74
  154.6 45.8 %reduce_sum.48 = bf16[8192,128]{1,0:T(8,128)(2,1)} reduce(bf16[8192,2,128]{2,1,0:T(2,128)(2,1)} %bitcast.115, bf16[]{:T(256)} %constant.18.clone.1), dimensions={1}, to_apply=%region_1.2 | reduce | flops 1048576 | bytes 6291458 | tf_op jit(solution)/shard_map/reduce_sum | solution.py:75
  200.5 7.7 %all-to-all-start = ((bf16[32,256,128]{2,1,0:T(8,128)(2,1)}), bf16[32,256,128]{2,1,0:T(8,128)(2,1)}, u32[]{:S(2)}, u32[]{:S(2)}) async-start(bf16[32,256,128]{2,1,0:T(8,128)(2,1)} %bitcast.116), calls=%async_computation | async-start | bytes 4194304 | tf_op jit(solution)/shard_map/all_to_all | solution.py:76
  208.1 0.2 reduce-scatter.2.cloned.1.call-start
  208.4 0.1 iota_add_fusion
  208.4 0.1 add.100
  208.5 0.8 dynamic_slice.7
  209.3 0.9 fusion.36
  210.2 0.0 reduce-scatter.2.cloned.1.call-update
  210.2 0.2 reduce-window.4
  210.4 0.2 select_reduce_fusion.1
  210.6 0.1 select_reduce_fusion
  210.7 42.6 %all-to-all-done = bf16[32,256,128]{2,1,0:T(8,128)(2,1)} async-done(((bf16[32,256,128]{2,1,0:T(8,128)(2,1)}), bf16[32,256,128]{2,1,0:T(8,128)(2,1)}, u32[]{:S(2)}, u32[]{:S(2)}) %all-to-all-start) | async-done | bytes 2097184 | tf_op jit(solution)/shard_map/all_to_all | solution.py:76
  253.3 6.6 %fusion.8 = f32[256,32,128]{2,0,1:T(8,128)} fusion(bf16[32,256,128]{2,1,0:T(8,128)(2,1)} %all-to-all-done, bf16[32,128,256]{2,1,0:T(8,128)(2,1)S(1)} %bitcast.112, bf16[256,4096]{1,0:T(8,128)(2,1)} %param.18), kind=kOutput, calls=%fused_computation.12 | convolution fusion | flops 1073807360 | bytes 10485760 | tf_op jit(solution)/shard_map/cr,rfd->fcd/dot_general | solution.py:84
  259.9 6.7 %fusion.18 = f32[256,1024]{1,0:T(8,128)S(1)} fusion(bf16[32,128,1024]{2,1,0:T(8,128)(2,1)} %bitcast.125, bf16[32,256,128]{2,1,0:T(8,128)(2,1)} %all-to-all-done, f32[256,32,128]{2,0,1:T(8,128)} %fusion.8, f32[32,128]{1,0:T(8,128)S(1)} %bitcast.118, f32[1024]{0:T(1024)S(1)} %copy-done.7), kind=kOutput, calls=%fused_computation.21 | convolution fusion | flops 2152988672 | bytes 15749120 | tf_op jit(solution)/shard_map/fcd,fdh->ch/dot_general | solution.py:86
  266.6 0.0 reduce-scatter.2.cloned.1.call-done
  266.6 1.1 fusion.47
  267.8 0.4 fusion.35
  268.2 0.3 copy-done.6
  268.5 7.1 %fusion.48 = f32[32,128,256]{1,2,0:T(8,128)} fusion(bf16[32,128,1024]{2,1,0:T(8,128)(2,1)} %bitcast.126, f32[256,1024]{1,0:T(8,128)S(1)} %fusion.18, f32[256]{0:T(256)S(1)} %maximum_divide_fusion, bf16[1,8,1024]{2,1,0:T(8,128)(2,1)S(1)} %copy-done.6, s32[8]{0:T(128)S(1)} %bitcast.124, s32[8]{0:T(128)S(1)} %fusion.65), kind=kOutput, calls=%fused_computation.39 | convolution fusion | flops 2154567680 | bytes 13648960 | tf_op jit(solution)/shard_map/ch,fdh->fcd/dot_general | solution.py:95
  275.6 9.6 %fusion.2 = bf16[32,256,128]{2,1,0:T(8,128)(2,1)} fusion(f32[32,128,256]{1,2,0:T(8,128)} %fusion.48, f32[256,32,128]{2,0,1:T(8,128)} %fusion.8, bf16[32,128,256]{2,1,0:T(8,128)(2,1)S(1)} %bitcast.113, f32[32,128]{1,0:T(8,128)S(1)} %bitcast.119, bf16[32,256,128]{2,1,0:T(8,128)(2,1)} %all-to-all-done, bf16[256,4096]{1,0:T(8,128)(2,1)} %param.18), kind=kOutput, calls=%fused_computation.6 | convolution fusion | flops 1082195968 | bytes 16793600 | tf_op jit(solution)/shard_map/cr,fdr->fcd/dot_general | solution.py:98
  285.2 53.3 %all_to_all.10 = bf16[32,256,128]{2,1,0:T(8,128)(2,1)S(1)} all-to-all(bf16[32,256,128]{2,1,0:T(8,128)(2,1)} %fusion.2), channel_id=1, replica_groups=mesh['dp'=8,'mp'=32] {'mp'}, dimensions={0} | all-to-all | bytes 4194304 | tf_op jit(solution)/shard_map/all_to_all | solution.py:100
  338.4 1.3 copy.43
  (23 shorter events, 0.1 us)
Async XLA Ops:
  7.2 246.1 %copy-start = (bf16[4096,256]{1,0:T(8,128)(2,1)S(1)}, bf16[4096,256]{1,0:T(8,128)(2,1)}, u32[]{:S(2)}) copy-start(bf16[4096,256]{1,0:T(8,128)(2,1)} %param.17) | copy-start | bytes 6291460
  7.2 82.1 %all-gather.3.cloned.1.call-start = ((), (), s32[]{:S(2)}) async-start(), calls=%async_computation.3 | async-start | bytes 1081344 | tf_op jit(solution)/shard_map/all_gather | solution.py:59
  8.8 251.1 %all-gather.5.cloned.1.call-start = ((), (), s32[]{:S(2)}) async-start(), calls=%async_computation.4 | async-start | bytes 9437184 | tf_op jit(solution)/shard_map/all_gather | solution.py:60
  92.7 4.1 %copy-start.1 = (bf16[1,2048,128]{2,1,0:T(8,128)(2,1)S(1)}, bf16[1,2048,128]{2,1,0:T(8,128)(2,1)}, u32[]{:S(2)}) copy-start(bf16[1,2048,128]{2,1,0:T(8,128)(2,1)} %param.11) | copy-start | bytes 1572868
  200.4 8.8 %copy-start.2 = (bf16[256,1024]{1,0:T(8,128)(2,1)S(1)}, bf16[256,1024]{1,0:T(8,128)(2,1)}, u32[]{:S(2)}) copy-start(bf16[256,1024]{1,0:T(8,128)(2,1)} %param.16) | copy-start | bytes 1572868
  200.5 9.8 %copy-start.8 = (s32[1,8]{1,0:T(1,128)S(1)}, s32[1,8]{1,0:T(1,128)}, u32[]{:S(2)}) copy-start(s32[1,8]{1,0:T(1,128)} %param.13) | copy-start | bytes 100
  200.5 10.0 %copy-start.4 = (s32[256]{0:T(256)S(1)}, s32[256]{0:T(256)}, u32[]{:S(2)}) copy-start(s32[256]{0:T(256)} %param.14) | copy-start | bytes 3076
  200.5 52.8 %all-to-all-start = ((bf16[32,256,128]{2,1,0:T(8,128)(2,1)}), bf16[32,256,128]{2,1,0:T(8,128)(2,1)}, u32[]{:S(2)}, u32[]{:S(2)}) async-start(bf16[32,256,128]{2,1,0:T(8,128)(2,1)} %bitcast.116), calls=%async_computation | async-start | bytes 4194304 | tf_op jit(solution)/shard_map/all_to_all | solution.py:76
  208.1 58.5 %reduce-scatter.2.cloned.1.call-start = ((), (), s32[]{:S(2)}) async-start(), calls=%async_computation.5 | async-start | bytes 147456 | tf_op jit(solution)/shard_map/reduce_scatter | solution.py:70
  253.3 6.6 %copy-start.3 = (f32[4096]{0:T(1024)S(1)}, f32[4096]{0:T(1024)}, u32[]{:S(2)}) copy-start(f32[4096]{0:T(1024)} %param.19) | copy-start | bytes 49156
  253.3 6.6 %copy-start.7 = (f32[1024]{0:T(1024)S(1)}, f32[1024]{0:T(1024)}, u32[]{:S(2)}) copy-start(f32[1024]{0:T(1024)} %param.21) | copy-start | bytes 12292
  267.8 0.7 copy-start.6
  267.8 7.8 %copy-start.5 = (f32[256]{0:T(256)}, f32[256]{0:T(256)S(1)}, u32[]{:S(2)}) copy-start(f32[256]{0:T(256)S(1)} %broadcast_multiply_fusion) | copy-start | bytes 3076
Sparse Core Ops, SparseCore 0:
  11.1 78.0 all-gather.2
  91.1 54.5 all-gather.4
  211.4 31.8 reduce-scatter.1
where the time goes:
time: 347 us; the launch traced here: 346 us
  waiting for transfers between devices  123 us (35%)
  local copies, waits for them, and re-layouts  69.3 us (20%)
  blocking collectives  53.3 us (15%)
  other arithmetic  46.4 us (13%)
  matrix products  32.4 us (9%)
  between operations  13.9 us (4%)
  starting transfers between devices  7.95 us (2%)
    all_gather x1, waiting for transfers between devices, local(): w_cols = lax.all_gather(w_piece, 'mp', axis=0, tiled=True)  80.5 us
    gather x1, local copies, waits for them, and re-layouts, local(): picked = jnp.take(slab, ids[:, 0, :], axis=0, mode='clip')  57.8 us
    all_to_all x1, blocking collectives, local(): lax.all_to_all(grads, 'mp', split_axis=0, concat_axis=0, tiled=True)  53.3 us
    reduce_sum x1, other arithmetic, local(): pooled = jnp.sum(picked.astype(f32), axis=1).astype(bf16)  45.8 us
    all_to_all x1, waiting for transfers between devices, local(): lax.all_to_all(pooled.reshape(n_mp, rows, emb), 'mp', split_axis=0, conca...  42.6 us
    dot_general x1, matrix products, local(): jnp.einsum('cr,fdr->fcd', dz, cd3, preferred_element_type=f32)  9.56 us
    all_to_all x1, starting transfers between devices, local(): lax.all_to_all(pooled.reshape(n_mp, rows, emb), 'mp', split_axis=0, conca...  7.65 us
    dot_general x1, matrix products, local(): dx1 = jnp.einsum('ch,fdh->fcd', dact, w3, preferred_element_type=f32)  7.13 us
  transfers between devices with their start and end apart: 4, of which 2 were waited for; matrix products, arithmetic and copies ran while one was open for 37% of the time, Pallas kernels for 0%

commit v1 on v0

--- a/solution.py
+++ b/solution.py
@@ -1,7 +1,45 @@
+import functools
 import jax
 import jax.numpy as jnp
 from jax import lax
 from jax.sharding import PartitionSpec as P
+
+
+def extend_the_ends(u_in, axis_tag):
+    all_values, finding, side_arr = (
+        lax.axis_size(axis_tag),
+        lax.axis_index(axis_tag),
+        u_in.shape[1],
+    )
+    sides = [
+        hop_no * all_values if src_i == 1 else hop_no for src_i, hop_no in enumerate(u_in.shape)
+    ]
+    built = state_next = u_in
+    work_now = lax.dynamic_update_slice_in_dim(
+        jnp.zeros(sides, u_in.dtype), u_in, finding * side_arr, axis=1
+    )
+    q = 1
+    while q < all_values // 2 + 1:
+        built = lax.ppermute(
+            built, axis_tag, [(src_i, (src_i + 1) % all_values) for src_i in range(all_values)]
+        )
+        work_now = lax.dynamic_update_slice_in_dim(
+            work_now, built, (finding - q) % all_values * side_arr, axis=1
+        )
+        if 2 * q < all_values:
+            state_next = lax.ppermute(
+                state_next,
+                axis_tag,
+                [(src_i, (src_i - 1) % all_values) for src_i in range(all_values)],
+            )
+            work_now = lax.dynamic_update_slice_in_dim(
+                work_now, state_next, (finding + q) % all_values * side_arr, axis=1
+            )
+        q += 1
+    return work_now
+
+
+cut_the_targets = functools.partial(extend_the_ends, axis_tag="dp")
 
 
 def members(counts_row, rows):
@@ -57,7 +95,7 @@
     piece = tower_weight.shape[1] // n_dp
     w_piece = lax.dynamic_slice_in_dim(tower_weight, d_idx * piece, piece, axis=1)
     w_cols = lax.all_gather(w_piece, "mp", axis=0, tiled=True)
-    w_all = lax.all_gather(w_cols, "dp", axis=1, tiled=True)
+    w_all = cut_the_targets(w_cols)
     w3 = w_all.reshape(n_mp, emb, width)
     held = user_codes.shape[0]
     home_local = lax.dynamic_slice_in_dim(request_home, d_idx * held, held)

time: 347 us -> 298 us (0.86)
  waiting for transfers between devices: 123 us -> 42.1 us
  local copies, waits for them, and re-layouts: 69.3 us -> 85.7 us
  starting transfers between devices: 7.95 us -> 15.9 us
  blocking collectives: 53.3 us -> 56.8 us
    all_gather x1, waiting for transfers between devices: 80.5 us -> 0.02 us  [local(): w_cols = lax.all_gather(w_piece, 'mp', axis=0, tiled=True)]
    all_to_all x1, waiting for transfers between devices: 42.6 us -> 17.6 us  [local(): lax.all_to_all(pooled.reshape(n_mp, rows, emb), 'mp', split_axis=0, conca...]
    ppermute x0 -> x7, waiting for transfers between devices: none -> 24.5 us  [the longest x4 18.4 us: extend_the_ends(): lax.ppermute(built, axis_tag, [(src_i, (src_i + 1) % all_values) for src_...]
    dynamic_update_slice x0 -> x8, local copies, waits for them, and re-layouts: none -> 12.9 us  [the longest x3 6.01 us: extend_the_ends(): lax.dynamic_update_slice_in_dim(work_now, state_next, (finding + q) % all...]
    broadcast_in_dim x0 -> x1, local copies, waits for them, and re-layouts: none -> 4.3 us  [extend_the_ends(): jnp.zeros(sides, u_in.dtype)]
    all_to_all x1, starting transfers between devices: 7.65 us -> 11.7 us  [local(): lax.all_to_all(pooled.reshape(n_mp, rows, emb), 'mp', split_axis=0, conca...]
    ppermute x0 -> x7, starting transfers between devices: none -> 3.98 us  [the longest x3 3.44 us: extend_the_ends(): lax.ppermute(state_next, axis_tag, [(src_i, (src_i - 1) % all_values) for...]
    all_to_all x1, blocking collectives: 53.3 us -> 56.8 us  [local(): lax.all_to_all(grads, 'mp', split_axis=0, concat_axis=0, tiled=True)]
  transfers between devices with their start and end apart: 4 -> 10, of which waited for: 2 -> 5; matrix products, arithmetic and copies ran while one was open for 37% -> 49% of each run, Pallas kernels for 0% -> 0%
where the time goes in v1:
time: 298 us
  local copies, waits for them, and re-layouts  85.7 us (29%)
  blocking collectives  56.8 us (19%)
  other arithmetic  46.4 us (16%)
  waiting for transfers between devices  42.1 us (14%)
  matrix products  34.9 us (12%)
  starting transfers between devices  15.9 us (5%)
  between operations  15.8 us (5%)
    gather x1, local copies, waits for them, and re-layouts, local(): picked = jnp.take(slab, ids[:, 0, :], axis=0, mode='clip')  57.4 us
    all_to_all x1, blocking collectives, local(): lax.all_to_all(grads, 'mp', split_axis=0, concat_axis=0, tiled=True)  56.8 us
    reduce_sum x1, other arithmetic, local(): pooled = jnp.sum(picked.astype(f32), axis=1).astype(bf16)  45.8 us
    ppermute x4, waiting for transfers between devices, extend_the_ends(): lax.ppermute(built, axis_tag, [(src_i, (src_i + 1) % all_values) for src_...  18.4 us
    all_to_all x1, waiting for transfers between devices, local(): lax.all_to_all(pooled.reshape(n_mp, rows, emb), 'mp', split_axis=0, conca...  17.6 us
    all_to_all x1, starting transfers between devices, local(): lax.all_to_all(pooled.reshape(n_mp, rows, emb), 'mp', split_axis=0, conca...  11.7 us
    dot_general x1, matrix products, local(): jnp.einsum('cr,fdr->fcd', dz, cd3, preferred_element_type=f32)  9.56 us
    dot_general x1, matrix products, local(): jnp.einsum('fcd,fdh->ch', x1, w3, preferred_element_type=f32) + tower_bias  7.44 us
  transfers between devices with their start and end apart: 10, of which 5 were waited for; matrix products, arithmetic and copies ran while one was open for 49% of the time, Pallas kernels for 0%

profile of v1, /device:TPU:10, one launch (start us, length us, event | category | flops | bytes accessed | tf_op | source)
XLA Modules:
  0.0 297.6 jit_solution(11523332863614143359)
XLA Ops:
  8.1 1.5 constant_dynamic-slice_fusion
  9.6 3.4 %copy.18 = s32[8192,1,2]{2,0,1:T(8,128)} copy(s32[8192,1,2]{0,2,1:T(2,128)} %param.12) | data formatting | bytes 131072 | tf_op args[1]
  13.0 4.0 %reshape.87 = s32[16384]{0:T(1024)S(1)} reshape(s32[8192,1,2]{2,0,1:T(8,128)} %copy.18) | data formatting | bytes 131072 | tf_op jit(solution)/shard_map/jit(_take)/broadcast_in_dim | solution.py:112
  17.1 57.4 %gather_fusion = bf16[16384,128]{1,0:T(8,128)(2,1)} fusion(bf16[2048,128]{1,0:T(8,128)(2,1)S(1)} %bitcast.114, s32[16384]{0:T(1024)S(1)} %broadcast_clamp_fusion), kind=kCustom, calls=%fused_computation | custom fusion | bytes 8454144 | tf_op jit(solution)/shard_map/jit(_take)/gather | solution.py:112
  74.4 45.8 %reduce_sum.48 = bf16[8192,128]{1,0:T(8,128)(2,1)} reduce(bf16[8192,2,128]{2,1,0:T(2,128)(2,1)} %bitcast.115, bf16[]{:T(256)} %constant.72.clone.1), dimensions={1}, to_apply=%region_1.2 | reduce | flops 1048576 | bytes 6291458 | tf_op jit(solution)/shard_map/reduce_sum | solution.py:113
  120.3 11.7 %all-to-all-start = ((bf16[32,256,128]{2,1,0:T(8,128)(2,1)}), bf16[32,256,128]{2,1,0:T(8,128)(2,1)}, u32[]{:S(2)}, u32[]{:S(2)}) async-start(bf16[32,256,128]{2,1,0:T(8,128)(2,1)} %bitcast.116), calls=%async_computation | async-start | bytes 4194304 | tf_op jit(solution)/shard_map/all_to_all | solution.py:114
  132.4 0.8 dynamic_slice.7
  133.2 1.9 fusion.36
  135.5 1.7 collective-permute-start.1
  137.4 9.3 %collective-permute-done = bf16[4096,128]{1,0:T(8,128)(2,1)S(1)} collective-permute-done((bf16[4096,128]{1,0:T(8,128)(2,1)}, bf16[4096,128]{1,0:T(8,128)(2,1)S(1)}, u32[]{:S(2)}, u32[]{:S(2)}) %collective-permute-start) | collective-permute-done | bytes 1048608 | tf_op jit(solution)/shard_map/ppermute | solution.py:23
  146.8 4.3 %broadcast_in_dim.29 = bf16[4096,1024]{1,0:T(8,128)(2,1)} broadcast(bf16[]{:T(256)} %constant.72.clone.1), dimensions={} | broadcast | bytes 8388610 | tf_op jit(solution)/shard_map/broadcast_in_dim | solution.py:19
  151.1 1.2 constant_dynamic-update-slice_fusion.7
  152.2 1.7 collective-permute-start.3
  154.0 1.1 constant_dynamic-update-slice_fusion.6
  155.1 6.2 %collective-permute-done.2 = bf16[4096,128]{1,0:T(8,128)(2,1)} collective-permute-done((bf16[4096,128]{1,0:T(8,128)(2,1)S(1)}, bf16[4096,128]{1,0:T(8,128)(2,1)}, u32[]{:S(2)}, u32[]{:S(2)}) %collective-permute-start.2) | collective-permute-done | bytes 1048608 | tf_op jit(solution)/shard_map/ppermute | solution.py:23
  161.3 2.3 constant_dynamic-update-slice_fusion.5
  163.7 17.6 %all-to-all-done = bf16[32,256,128]{2,1,0:T(8,128)(2,1)} async-done(((bf16[32,256,128]{2,1,0:T(8,128)(2,1)}), bf16[32,256,128]{2,1,0:T(8,128)(2,1)}, u32[]{:S(2)}, u32[]{:S(2)}) %all-to-all-start) | async-done | bytes 2097184 | tf_op jit(solution)/shard_map/all_to_all | solution.py:114
  181.3 6.5 %fusion.8 = f32[256,32,128]{2,0,1:T(8,128)} fusion(bf16[32,256,128]{2,1,0:T(8,128)(2,1)} %all-to-all-done, bf16[32,128,256]{2,1,0:T(8,128)(2,1)S(1)} %bitcast.112, bf16[256,4096]{1,0:T(8,128)(2,1)} %param.18), kind=kOutput, calls=%fused_computation.12 | convolution fusion | flops 1073807360 | bytes 10485760 | tf_op jit(solution)/shard_map/cr,rfd->fcd/dot_general | solution.py:122
  187.8 2.4 constant_dynamic-update-slice_fusion.4
  190.2 0.5 collective-permute-start.6
  190.7 2.6 constant_dynamic-update-slice_fusion.3
  193.3 1.1 constant_dynamic-update-slice_fusion.2
  194.4 6.1 %collective-permute-done.5 = bf16[4096,128]{1,0:T(8,128)(2,1)S(1)} collective-permute-done((bf16[4096,128]{1,0:T(8,128)(2,1)}, bf16[4096,128]{1,0:T(8,128)(2,1)S(1)}, u32[]{:S(2)}, u32[]{:S(2)}) %collective-permute-start.5) | collective-permute-done | bytes 1048608 | tf_op jit(solution)/shard_map/ppermute | solution.py:30
  200.4 1.1 constant_dynamic-update-slice_fusion.1
  201.6 2.9 collective-permute-done.6
  204.4 1.1 constant_dynamic-update-slice_fusion
  205.5 7.4 %fusion.18 = f32[256,1024]{1,0:T(8,128)} fusion(bf16[32,128,1024]{2,1,0:T(8,128)(2,1)} %bitcast.12, bf16[32,256,128]{2,1,0:T(8,128)(2,1)} %all-to-all-done, f32[256,32,128]{2,0,1:T(8,128)S(1)} %copy-done.2, f32[32,128]{1,0:T(8,128)S(1)} %bitcast.118, f32[1024]{0:T(1024)S(1)} %copy-done.8), kind=kOutput, calls=%fused_computation.21 | convolution fusion | flops 2152988672 | bytes 15749120 | tf_op jit(solution)/shard_map/fcd,fdh->ch/dot_general | solution.py:124
  213.0 1.6 fusion.47
  215.1 7.4 %fusion.48 = f32[32,128,256]{1,2,0:T(8,128)} fusion(bf16[32,128,1024]{2,1,0:T(8,128)(2,1)} %bitcast.12, f32[256,1024]{1,0:T(8,128)} %fusion.18, f32[256]{0:T(256)S(1)} %maximum_divide_fusion, bf16[1,8,1024]{2,1,0:T(8,128)(2,1)S(1)} %copy-done.7, s32[8]{0:T(128)S(1)} %bitcast.124, s32[8]{0:T(128)S(1)} %fusion.65), kind=kOutput, calls=%fused_computation.39 | convolution fusion | flops 2154567680 | bytes 13648960 | tf_op jit(solution)/shard_map/ch,fdh->fcd/dot_general | solution.py:133
  222.5 9.6 %fusion.2 = bf16[32,256,128]{2,1,0:T(8,128)(2,1)} fusion(f32[32,128,256]{1,2,0:T(8,128)} %fusion.48, f32[256,32,128]{2,0,1:T(8,128)} %fusion.8, bf16[32,128,256]{2,1,0:T(8,128)(2,1)S(1)} %bitcast.113, f32[32,128]{1,0:T(8,128)S(1)} %bitcast.119, bf16[32,256,128]{2,1,0:T(8,128)(2,1)} %all-to-all-done, bf16[256,4096]{1,0:T(8,128)(2,1)} %param.18), kind=kOutput, calls=%fused_computation.6 | convolution fusion | flops 1082195968 | bytes 16793600 | tf_op jit(solution)/shard_map/cr,fdr->fcd/dot_general | solution.py:136
  232.0 56.8 %all_to_all.10 = bf16[32,256,128]{2,1,0:T(8,128)(2,1)S(1)} all-to-all(bf16[32,256,128]{2,1,0:T(8,128)(2,1)} %fusion.2), channel_id=1, replica_groups=mesh['dp'=8,'mp'=32] {'mp'}, dimensions={0} | all-to-all | bytes 4194304 | tf_op jit(solution)/shard_map/all_to_all | solution.py:138
  288.8 1.3 copy.51
  (45 shorter events, 1.4 us)
Async XLA Ops:
  8.0 173.3 %copy-start = (bf16[4096,256]{1,0:T(8,128)(2,1)S(1)}, bf16[4096,256]{1,0:T(8,128)(2,1)}, u32[]{:S(2)}) copy-start(bf16[4096,256]{1,0:T(8,128)(2,1)} %param.17) | copy-start | bytes 6291460
  8.0 124.2 %all-gather.2.cloned.1.call-start = ((), (), s32[]{:S(2)}) async-start(), calls=%async_computation.3 | async-start | bytes 1081344 | tf_op jit(solution)/shard_map/all_gather | solution.py:97
  9.6 7.5 %copy-start.1 = (bf16[1,2048,128]{2,1,0:T(8,128)(2,1)S(1)}, bf16[1,2048,128]{2,1,0:T(8,128)(2,1)}, u32[]{:S(2)}) copy-start(bf16[1,2048,128]{2,1,0:T(8,128)(2,1)} %param.11) | copy-start | bytes 1572868
  74.4 60.8 %copy-start.9 = (s32[1,8]{1,0:T(1,128)S(1)}, s32[1,8]{1,0:T(1,128)}, u32[]{:S(2)}) copy-start(s32[1,8]{1,0:T(1,128)} %param.13) | copy-start | bytes 100
  74.4 62.7 %copy-start.5 = (s32[256]{0:T(256)S(1)}, s32[256]{0:T(256)}, u32[]{:S(2)}) copy-start(s32[256]{0:T(256)} %param.14) | copy-start | bytes 3076
  120.3 61.0 %all-to-all-start = ((bf16[32,256,128]{2,1,0:T(8,128)(2,1)}), bf16[32,256,128]{2,1,0:T(8,128)(2,1)}, u32[]{:S(2)}, u32[]{:S(2)}) async-start(bf16[32,256,128]{2,1,0:T(8,128)(2,1)} %bitcast.116), calls=%async_computation | async-start | bytes 4194304 | tf_op jit(solution)/shard_map/all_to_all | solution.py:114
  132.0 81.0 %reduce-scatter.2.cloned.1.call-start = ((), (), s32[]{:S(2)}) async-start(), calls=%async_computation.4 | async-start | bytes 147456 | tf_op jit(solution)/shard_map/reduce_scatter | solution.py:108
  132.2 14.4 %collective-permute-start = (bf16[4096,128]{1,0:T(8,128)(2,1)}, bf16[4096,128]{1,0:T(8,128)(2,1)S(1)}, u32[]{:S(2)}, u32[]{:S(2)}) collective-permute-start(bf16[4096,128]{1,0:T(8,128)(2,1)} %all-gather.2.cloned.1.call-done), channel_id=1, source_target_pairs={{0,32},{32,64},{64,96},{96,128},{128,160},{160,192},{192,224},{224... | collective-permute-start | bytes 3145736 | tf_op jit(solution)/shard_map/ppermute | solution.py:23
  135.5 16.8 %collective-permute-start.1 = (bf16[4096,128]{1,0:T(8,128)(2,1)}, bf16[4096,128]{1,0:T(8,128)(2,1)}, u32[]{:S(2)}, u32[]{:S(2)}) collective-permute-start(bf16[4096,128]{1,0:T(8,128)(2,1)} %all-gather.2.cloned.1.call-done), channel_id=1, source_target_pairs={{0,224},{32,0},{64,32},{96,64},{128,96},{160,128},{192,160},{224,1... | collective-permute-start | bytes 3145736 | tf_op jit(solution)/shard_map/ppermute | solution.py:30
  146.7 14.7 %collective-permute-start.2 = (bf16[4096,128]{1,0:T(8,128)(2,1)S(1)}, bf16[4096,128]{1,0:T(8,128)(2,1)}, u32[]{:S(2)}, u32[]{:S(2)}) collective-permute-start(bf16[4096,128]{1,0:T(8,128)(2,1)S(1)} %collective-permute-done), channel_id=1, source_target_pairs={{0,32},{32,64},{64,96},{96,128},{128,160},{160,192},{192,224},{224... | collective-permute-start | bytes 3145736 | tf_op jit(solution)/shard_map/ppermute | solution.py:23
  146.8 4.3 %copy-start.3 = (bf16[4096,128]{1,0:T(8,128)(2,1)S(1)}, bf16[4096,128]{1,0:T(8,128)(2,1)}, u32[]{:S(2)}) copy-start(bf16[4096,128]{1,0:T(8,128)(2,1)} %all-gather.2.cloned.1.call-done) | copy-start | bytes 3145732
  152.2 35.6 %collective-permute-start.3 = (bf16[4096,128]{1,0:T(8,128)(2,1)}, bf16[4096,128]{1,0:T(8,128)(2,1)}, u32[]{:S(2)}, u32[]{:S(2)}) collective-permute-start(bf16[4096,128]{1,0:T(8,128)(2,1)} %collective-permute-done.1), channel_id=1, source_target_pairs={{0,224},{32,0},{64,32},{96,64},{128,96},{160,128},{192,160},{224,1... | collective-permute-start | bytes 3145736 | tf_op jit(solution)/shard_map/ppermute | solution.py:30
  161.3 28.9 %collective-permute-start.4 = (bf16[4096,128]{1,0:T(8,128)(2,1)}, bf16[4096,128]{1,0:T(8,128)(2,1)S(1)}, u32[]{:S(2)}, u32[]{:S(2)}) collective-permute-start(bf16[4096,128]{1,0:T(8,128)(2,1)} %collective-permute-done.2), channel_id=1, source_target_pairs={{0,32},{32,64},{64,96},{96,128},{128,160},{160,192},{192,224},{224... | collective-permute-start | bytes 3145736 | tf_op jit(solution)/shard_map/ppermute | solution.py:23
  187.8 12.6 %collective-permute-start.5 = (bf16[4096,128]{1,0:T(8,128)(2,1)}, bf16[4096,128]{1,0:T(8,128)(2,1)S(1)}, u32[]{:S(2)}, u32[]{:S(2)}) collective-permute-start(bf16[4096,128]{1,0:T(8,128)(2,1)} %collective-permute-done.3), channel_id=1, source_target_pairs={{0,224},{32,0},{64,32},{96,64},{128,96},{160,128},{192,160},{224,1... | collective-permute-start | bytes 3145736 | tf_op jit(solution)/shard_map/ppermute | solution.py:30
  190.2 15.3 %copy-start.2 = (f32[256,32,128]{2,0,1:T(8,128)S(1)}, f32[256,32,128]{2,0,1:T(8,128)}, u32[]{:S(2)}) copy-start(f32[256,32,128]{2,0,1:T(8,128)} %fusion.8) | copy-start | bytes 12582916
  190.2 15.3 %copy-start.4 = (f32[4096]{0:T(1024)S(1)}, f32[4096]{0:T(1024)}, u32[]{:S(2)}) copy-start(f32[4096]{0:T(1024)} %param.19) | copy-start | bytes 49156
  190.2 15.3 %copy-start.8 = (f32[1024]{0:T(1024)S(1)}, f32[1024]{0:T(1024)}, u32[]{:S(2)}) copy-start(f32[1024]{0:T(1024)} %param.21) | copy-start | bytes 12292
  190.2 14.2 %collective-permute-start.6 = (bf16[4096,128]{1,0:T(8,128)(2,1)S(1)}, bf16[4096,128]{1,0:T(8,128)(2,1)S(1)}, u32[]{:S(2)}, u32[]{:S(2)}) collective-permute-start(bf16[4096,128]{1,0:T(8,128)(2,1)S(1)} %collective-permute-done.4), channel_id=1, source_target_pairs={{0,32},{32,64},{64,96},{96,128},{128,160},{160,192},{192,224},{224... | collective-permute-start | bytes 3145736 | tf_op jit(solution)/shard_map/ppermute | solution.py:23
  213.0 2.1 copy-start.7
  214.6 7.8 %copy-start.6 = (f32[256]{0:T(256)}, f32[256]{0:T(256)S(1)}, u32[]{:S(2)}) copy-start(f32[256]{0:T(256)S(1)} %broadcast_multiply_fusion) | copy-start | bytes 3076
Sparse Core Ops, SparseCore 0:
  11.4 78.0 all-gather.1
Sparse Core Ops, SparseCore 1:
  135.2 32.9 reduce-scatter.1
